TPU v7x, 32 devices: a whole 2x2x4 slice. The times are simulated.
32 devices in a mesh: groups: 2 (over x), seq: 8 (over z, y), chan: 2 (over core).
Axes of the slice: x: 2, y: 2, z: 4, core: 2. Of those that a mesh axis runs over, the one named last changes fastest.
Arguments:
- cached_input: bfloat16 [2048, 4096], P(('groups', 'seq'), 'chan'), parts along dimension 0, may hold values from -6 to 6
- cached_gate: bfloat16 [2048, 4096], P(('groups', 'seq'), 'chan'), parts along dimension 0, may hold values from -6 to 6
- out_grad: bfloat16 [2048, 4096], P(('groups', 'seq'), 'chan'), parts along dimension 0, may hold values from -1.75 to 1.75
- filter_taps: bfloat16 [1024, 32], P('seq', 'chan'), may hold values from -6 to 6
- skip_gain: float32 [4096], P('chan'), may hold values from -1 to 1
Outputs:
- input_grad: bfloat16 [2048, 4096], P(('groups', 'seq'), 'chan'), parts along dimension 0
- filter_grad: float32 [2048, 32], P(('groups', 'seq'), 'chan'), parts along dimension 0
There are 2 independent parts, one for each index of `groups`. A program takes and returns all parts, laid end to end along the dimension named above; an argument that names none is the same for every part. Nothing has to cross between parts.
All inputs are finite; a program needn't handle non-finite values.
Results may differ from a plain program's by a relative error of at most 0.005.
Values may be sent and summed in bfloat16 or wider, within the bound.
No kernel may reach another device: no remote copies, remote signals or barrier semaphores. Data moves between devices by JAX's collectives and lax.ppermute only.
A program may use at most 64 MiB of HBM per device.

v0:
```python
import math
import jax
import numpy as np
import jax.numpy as jnp
from jax import lax
from jax.sharding import PartitionSpec as P

lag_group = 4


def toeplitz_blocks(windows, block_rows):
    flipped = windows[..., ::-1]
    tiled = jnp.tile(flipped, (1, 1, block_rows))
    trimmed = tiled[..., : block_rows * (2 * block_rows - 1)]
    shaped = trimmed.reshape(windows.shape[0], windows.shape[1], block_rows, 2 * block_rows - 1)
    return shaped[..., block_rows - 1 : 2 * block_rows - 1]


def diagonal_sums(products, block_rows):
    flipped = products[..., ::-1]
    padded = jnp.pad(flipped, ((0, 0), (0, 0), (0, 0), (0, block_rows)))
    flattened = padded.reshape(products.shape[0], products.shape[1], 2 * block_rows * block_rows)
    trimmed = flattened[..., : block_rows * (2 * block_rows - 1)]
    shaped = trimmed.reshape(products.shape[0], products.shape[1], block_rows, 2 * block_rows - 1)
    diag_sums = jnp.sum(shaped, axis=2)
    return jnp.pad(diag_sums, ((0, 0), (0, 0), (1, 0)))


def fold_windows(window_grads, block_rows):
    front_half = jnp.pad(window_grads[..., :block_rows], ((0, 1), (0, 0), (0, 0)))
    back_half = jnp.pad(window_grads[..., block_rows:], ((1, 0), (0, 0), (0, 0)))
    joined = front_half + back_half
    return jnp.transpose(joined, (1, 0, 2)).reshape(window_grads.shape[1], -1)


def lag_table(taps_all, block_rows):
    return jnp.pad(jnp.transpose(taps_all), ((0, 0), (block_rows, lag_group * block_rows)))


def lag_sweep(
    blocks, base_block, block_count, sources, tap_table, block_rows, trip_count, seq_count
):
    filters = sources.shape[2]
    group_width = sources.shape[3]

    def advance(lag_step, state_pair):
        input_acc, lag_acc = state_pair
        lag_start = lag_step * lag_group
        stacked = jnp.stack(
            [
                lax.dynamic_slice_in_dim(blocks, base_block + lag_start + offset, block_count, 0)
                for offset in range(lag_group)
            ],
            axis=1,
        )
        lag_span = lax.dynamic_slice_in_dim(
            tap_table, lag_start * block_rows, (lag_group + 1) * block_rows, 1
        )
        windows = jnp.stack(
            [
                lag_span[:, offset * block_rows : (offset + 2) * block_rows]
                for offset in range(lag_group)
            ],
            axis=0,
        )
        toeplitz = toeplitz_blocks(windows, block_rows)
        input_acc = input_acc + jnp.einsum(
            "kfts,iktfg->isfg", toeplitz, stacked, preferred_element_type=jnp.float32
        )
        products = jnp.einsum(
            "iktfg,isfg->kfts", stacked, sources, preferred_element_type=jnp.float32
        )
        folded = fold_windows(diagonal_sums(products, block_rows), block_rows)
        previous = lax.dynamic_slice_in_dim(
            lag_acc, lag_start * block_rows, (lag_group + 1) * block_rows, 1
        )
        lag_acc = lax.dynamic_update_slice_in_dim(
            lag_acc, previous + folded, lag_start * block_rows, 1
        )
        return (input_acc, lag_acc)

    initial = (
        jnp.zeros((block_count, block_rows, filters, group_width), jnp.float32),
        jnp.zeros((filters, (seq_count + 1 + lag_group) * block_rows), jnp.float32),
    )
    return lax.fori_loop(0, trip_count, advance, initial)


def per_device(cached_input, cached_gate, out_grad, filter_taps, skip_gain):
    block_rows = cached_input.shape[0]
    chan_width = cached_input.shape[1]
    filters = filter_taps.shape[1]
    group_width = chan_width // filters
    seq_count = lax.axis_size("seq")
    seq_index = lax.axis_index("seq")
    length = block_rows * seq_count
    taps_scale = 1.0 / math.sqrt(length)
    gated_grad = (out_grad.astype(jnp.float32) * cached_gate.astype(jnp.float32)).astype(
        jnp.bfloat16
    )
    stretch_width = chan_width // seq_count
    stretch_filters = max(1, stretch_width // group_width)
    stretch_group = stretch_width // stretch_filters
    first_filter = seq_index * stretch_width // group_width
    tap_columns = np.array(
        [
            target * stretch_width // group_width + offset
            for target in range(seq_count)
            for offset in range(stretch_filters)
        ]
    )
    routed_taps = filter_taps[:, tap_columns].reshape(block_rows, seq_count, stretch_filters)
    packed = jnp.concatenate(
        [
            gated_grad.reshape(block_rows, seq_count, stretch_width),
            cached_input.reshape(block_rows, seq_count, stretch_width),
            routed_taps,
        ],
        axis=2,
    )
    moved = lax.all_to_all(packed, "seq", split_axis=1, concat_axis=0, tiled=True)
    moved = moved.reshape(length, 2 * stretch_width + stretch_filters)
    moved_grad = moved[:, :stretch_width]
    moved_input = moved[:, stretch_width : 2 * stretch_width]
    stretch_taps = moved[:, 2 * stretch_width :]
    shaped_grad = moved_grad.reshape(seq_count, block_rows, stretch_filters, stretch_group)
    blocks = jnp.pad(shaped_grad, ((0, seq_count - 1 + lag_group), (0, 0), (0, 0), (0, 0)))
    sources = moved_input.reshape(seq_count, block_rows, stretch_filters, stretch_group)
    trip_count = (seq_count + lag_group - 1) // lag_group
    input_acc, lag_acc = lag_sweep(
        blocks,
        0,
        seq_count,
        sources,
        lag_table(stretch_taps, block_rows),
        block_rows,
        trip_count,
        seq_count,
    )
    stretch_gain = lax.dynamic_slice_in_dim(skip_gain, seq_index * stretch_width, stretch_width, 0)
    conv_grad = input_acc.reshape(length, stretch_width) * taps_scale
    local_grad = (conv_grad + stretch_gain[None, :] * moved_grad.astype(jnp.float32)).astype(
        jnp.bfloat16
    )
    input_grad = lax.all_to_all(local_grad, "seq", split_axis=0, concat_axis=1, tiled=True)
    stretch_term = jnp.transpose(lag_acc[:, block_rows : block_rows + length]) * taps_scale
    lag_parts = lax.all_to_all(
        stretch_term.reshape(seq_count, block_rows, stretch_filters),
        "seq",
        split_axis=0,
        concat_axis=0,
        tiled=True,
    )
    sharers = seq_count * stretch_filters // filters
    filter_grad = (
        jnp.transpose(lag_parts, (1, 0, 2)).reshape(block_rows, filters, sharers).sum(axis=2)
    )
    return (input_grad, filter_grad)


def solution(mesh):
    return jax.shard_map(
        per_device,
        mesh=mesh,
        in_specs=(
            P(("groups", "seq"), "chan"),
            P(("groups", "seq"), "chan"),
            P(("groups", "seq"), "chan"),
            P("seq", "chan"),
            P("chan"),
        ),
        out_specs=(P(("groups", "seq"), "chan"), P(("groups", "seq"), "chan")),
        check_vma=False,
    )
```

profile of v0, /device:TPU:0, one launch (start us, length us, event | category | flops | bytes accessed | tf_op | source)
XLA Modules:
  0.0 98.7 jit_solution(5453652676311803673)
XLA Ops:
  0.7 1.4 %copy.32 = bf16[128,2048]{0,1:T(8,128)(2,1)S(1)} copy(bf16[128,2048]{1,0:T(8,128)(2,1)} %param.9) | data formatting | bytes 1048576 | tf_op args[0]
  3.1 1.1 %pad_maximum_fusion.4 = bf16[128,8,514]{0,2,1:T(8,128)(2,1)} fusion(bf16[128,8,2]{0,2,1:T(2,128)(2,1)S(1)} %bitcast.138, bf16[128,8,256]{0,2,1:T(8,128)(2,1)S(1)} %bitcast.136, bf16[128,8,256]{0,2,1:T(8,128)(2,1)S(1)} %bitcast.137), kind=kLoop, calls=%fused_computation.25 | loop fusion | flops 3158016 | bytes 2105344 | tf_op jit(solution)/shard_map/concatenate | solution.py:113
  4.2 7.3 %all-to-all-start = ((bf16[128,8,514]{0,2,1:T(8,128)(2,1)}), bf16[128,8,514]{0,2,1:T(8,128)(2,1)S(1)}, u32[]{:S(2)}, u32[]{:S(2)}) async-start(bf16[128,8,514]{0,2,1:T(8,128)(2,1)} %pad_maximum_fusion.4), calls=%async_computation | async-start | bytes 2129920 | tf_op jit(solution)/shard_map/all_to_all | solution.py:121
  12.2 25.4 %all-to-all-done = bf16[128,8,514]{0,2,1:T(8,128)(2,1)S(1)} async-done(((bf16[128,8,514]{0,2,1:T(8,128)(2,1)}), bf16[128,8,514]{0,2,1:T(8,128)(2,1)S(1)}, u32[]{:S(2)}, u32[]{:S(2)}) %all-to-all-start) | async-done | bytes 1052704 | tf_op jit(solution)/shard_map/all_to_all | solution.py:121
  39.5 1.1 %copy.35 = bf16[8,128,2,128]{3,1,0,2:T(8,128)(2,1)} copy(bf16[8,128,2,128]{1,0,3,2:T(8,128)(2,1)S(1)} %bitcast.135) | data formatting | bytes 1048576
  40.6 26.8 %while.18 = (s32[]{:T(128)}, f32[8,128,2,128]{1,3,0,2:T(8,128)}, f32[2,1664]{1,0:T(2,128)S(1)}, bf16[19,128,2,128]{1,3,0,2:T(8,128)(2,1)S(1)}, bf16[2,1664]{1,0:...) while((s32[]{:T(128)}, f32[8,128,2,128]{1,3,0,2:T(8,128)}, ...), condition=%wide.region_2.3_spmd.clone, body=%wide.region_0.2_spmd.clone.sunk | while | flops 543954432 | bytes 31783416 | solution.py:86
  40.6 1.2 %dynamic-slice_bitcast_fusion.5 = (bf16[8,1,128,2,128]{2,4,1,0,3:T(8,128)(2,1)S(1)}, bf16[8,1,128,2,128]{2,4,1,0,3:T(8,128)(2,1)S(1)}, bf16[8,1,128,2,128]{2,4,1,0,3:T(8,128)(2,1)}, bf16[8,1,128,2,128]{2,4,1,0,3:T(8,128)(2,1)}) fusion(bf16[19,128,2,128]{1,3,0,2:T(8,128)(2,1)S(1)} %get-tuple-element.324, s32[]{:T(128)S(6)} %select_n.70, ...), kind=kLoop, calls=%fused_computation.9.clone.1 | loop fusion | bytes 4194320 | tf_op jit(solution)/shard_map/while/body/eval_jaxpr/stack | solution.py:49
  42.6 1.6 %reshape.107 = bf16[4,2,128,255]{3,2,1,0:T(8,128)(2,1)S(1)} reshape(bf16[4,2,32640]{2,1,0:T(2,128)(2,1)S(1)} %slice.144) | data formatting | bytes 1044480 | tf_op jit(solution)/shard_map/while/body/eval_jaxpr/reshape | solution.py:15
  44.2 3.1 %fusion.21 = f32[8,128,2,128]{1,3,0,2:T(8,128)} fusion(f32[8,128,2,128]{1,3,0,2:T(8,128)} %get-tuple-element.301, pred[]{:T(512)S(6)} %compare.9, bf16[8,1,128,2,128]{2,4,1,0,3:T(8,128)(2,1)S(1)} %get-tuple-element.269, bf16[8,1,128,2,128]{2,4,1,0,3:T(8,128)(2,1)} %get-tuple-element.270, bf16[8,1,128,2,128]{2,4,1,0,3:T(8,128)(2,1)} %get-tuple-element.271, ...), kind=kOutput, calls=%fused_computation.3.clone.1 | convolution fusion | flops 272105472 | bytes 4456449 | tf_op jit(solution)/shard_map/while/body/eval_jaxpr/kfts,iktfg->isfg/dot_general | solution.py:67
  47.3 1.1 %convolution_bitcast_fusion.3 = f32[4,2,128,128]{3,2,0,1:T(8,128)S(1)} fusion(bf16[8,128,2,128]{3,1,0,2:T(8,128)(2,1)S(1)} %copy-done.6, bf16[8,1,128,2,128]{2,4,1,0,3:T(8,128)(2,1)S(1)} %get-tuple-element.269, bf16[8,1,128,2,128]{2,4,1,0,3:T(8,128)(2,1)S(1)} %copy-done.1, bf16[8,1,128,2,128]{2,4,1,0,3:T(8,128)(2,1)S(1)} %copy-done.2, ...), kind=kOutput, calls=%fused_computation.4.clone.1 | convolution fusion | flops 271581184 | bytes 3145728 | tf_op jit(solution)/shard_map/while/body/eval_jaxpr/iktfg,isfg->kfts/dot_general | solution.py:70
  49.8 1.0 %slice.145 = f32[4,2,32640]{2,0,1:T(4,128)} slice(f32[4,2,32768]{2,0,1:T(4,128)S(1)} %reshape.108), slice={[0:4], [0:2], [0:32640]} | slice | bytes 2088960 | tf_op jit(solution)/shard_map/while/body/eval_jaxpr/slice | solution.py:23
  50.8 2.8 %reshape.109 = f32[4,2,128,255]{3,2,0,1:T(8,128)S(1)} reshape(f32[4,2,32640]{2,0,1:T(4,128)} %slice.145) | data formatting | bytes 2088960 | tf_op jit(solution)/shard_map/while/body/eval_jaxpr/reshape | solution.py:24
  53.9 1.2 %dynamic-slice_bitcast_fusion.5 = (bf16[8,1,128,2,128]{2,4,1,0,3:T(8,128)(2,1)S(1)}, bf16[8,1,128,2,128]{2,4,1,0,3:T(8,128)(2,1)S(1)}, bf16[8,1,128,2,128]{2,4,1,0,3:T(8,128)(2,1)}, bf16[8,1,128,2,128]{2,4,1,0,3:T(8,128)(2,1)}) fusion(bf16[19,128,2,128]{1,3,0,2:T(8,128)(2,1)S(1)} %get-tuple-element.324, s32[]{:T(128)S(6)} %select_n.70, ...), kind=kLoop, calls=%fused_computation.9.clone.1 | loop fusion | bytes 4194320 | tf_op jit(solution)/shard_map/while/body/eval_jaxpr/stack | solution.py:49
  55.8 1.6 %reshape.107 = bf16[4,2,128,255]{3,2,1,0:T(8,128)(2,1)S(1)} reshape(bf16[4,2,32640]{2,1,0:T(2,128)(2,1)S(1)} %slice.144) | data formatting | bytes 1044480 | tf_op jit(solution)/shard_map/while/body/eval_jaxpr/reshape | solution.py:15
  57.4 3.5 %fusion.21 = f32[8,128,2,128]{1,3,0,2:T(8,128)} fusion(f32[8,128,2,128]{1,3,0,2:T(8,128)} %get-tuple-element.301, pred[]{:T(512)S(6)} %compare.9, bf16[8,1,128,2,128]{2,4,1,0,3:T(8,128)(2,1)S(1)} %get-tuple-element.269, bf16[8,1,128,2,128]{2,4,1,0,3:T(8,128)(2,1)} %get-tuple-element.270, bf16[8,1,128,2,128]{2,4,1,0,3:T(8,128)(2,1)} %get-tuple-element.271, ...), kind=kOutput, calls=%fused_computation.3.clone.1 | convolution fusion | flops 272105472 | bytes 4456449 | tf_op jit(solution)/shard_map/while/body/eval_jaxpr/kfts,iktfg->isfg/dot_general | solution.py:67
  60.9 1.1 %convolution_bitcast_fusion.3 = f32[4,2,128,128]{3,2,0,1:T(8,128)S(1)} fusion(bf16[8,128,2,128]{3,1,0,2:T(8,128)(2,1)S(1)} %copy-done.6, bf16[8,1,128,2,128]{2,4,1,0,3:T(8,128)(2,1)S(1)} %get-tuple-element.269, bf16[8,1,128,2,128]{2,4,1,0,3:T(8,128)(2,1)S(1)} %copy-done.1, bf16[8,1,128,2,128]{2,4,1,0,3:T(8,128)(2,1)S(1)} %copy-done.2, ...), kind=kOutput, calls=%fused_computation.4.clone.1 | convolution fusion | flops 271581184 | bytes 3145728 | tf_op jit(solution)/shard_map/while/body/eval_jaxpr/iktfg,isfg->kfts/dot_general | solution.py:70
  63.4 1.0 %slice.145 = f32[4,2,32640]{2,0,1:T(4,128)} slice(f32[4,2,32768]{2,0,1:T(4,128)S(1)} %reshape.108), slice={[0:4], [0:2], [0:32640]} | slice | bytes 2088960 | tf_op jit(solution)/shard_map/while/body/eval_jaxpr/slice | solution.py:23
  64.4 2.8 %reshape.109 = f32[4,2,128,255]{3,2,0,1:T(8,128)S(1)} reshape(f32[4,2,32640]{2,0,1:T(4,128)} %slice.145) | data formatting | bytes 2088960 | tf_op jit(solution)/shard_map/while/body/eval_jaxpr/reshape | solution.py:24
  67.5 1.3 %broadcast_multiply_fusion = f32[8,128,2,128]{1,3,0,2:T(8,128)S(1)} fusion(f32[8,128,2,128]{1,3,0,2:T(8,128)} %get-tuple-element.161), kind=kLoop, calls=%fused_computation.33 | loop fusion | flops 262144 | bytes 2097152 | tf_op jit(solution)/shard_map/mul | solution.py:141
  70.0 3.6 %all-to-all-start.2 = ((f32[8,128,2]{1,2,0:T(2,128)}), f32[8,128,2]{1,2,0:T(2,128)S(1)}, u32[]{:S(2)}, u32[]{:S(2)}) async-start(f32[8,128,2]{1,2,0:T(2,128)} %multiply_bitcast_fusion), calls=%async_computation.2 | async-start | bytes 16384 | tf_op jit(solution)/shard_map/all_to_all | solution.py:147
  73.6 2.1 %copy_bitcast_fusion.3 = bf16[8,128,256]{1,2,0:T(8,128)(2,1)} fusion(f32[32,8,8,128]{3,2,1,0:T(8,128)S(1)} %bitcast.132, f32[256]{0:T(256)S(1)} %dynamic_slice.63, bf16[1024,514]{0,1:T(8,128)(2,1)} %bitcast.128), kind=kLoop, calls=%fused_computation.31 | loop fusion | flops 1048576 | bytes 2098176 | tf_op jit(solution)/shard_map/all_to_all | solution.py:145
  75.7 4.4 %all-to-all-done.2 = f32[8,128,2]{1,2,0:T(2,128)S(1)} async-done(((f32[8,128,2]{1,2,0:T(2,128)}), f32[8,128,2]{1,2,0:T(2,128)S(1)}, u32[]{:S(2)}, u32[]{:S(2)}) %all-to-all-start.2) | async-done | bytes 8224 | tf_op jit(solution)/shard_map/all_to_all | solution.py:147
  80.1 3.5 %all-to-all-start.1 = ((bf16[8,128,256]{1,2,0:T(8,128)(2,1)}), bf16[8,128,256]{1,2,0:T(8,128)(2,1)S(1)}, u32[]{:S(2)}, u32[]{:S(2)}) async-start(bf16[8,128,256]{1,2,0:T(8,128)(2,1)} %copy_bitcast_fusion.3), calls=%async_computation.1 | async-start | bytes 1048576 | tf_op jit(solution)/shard_map/all_to_all | solution.py:145
  83.6 13.4 %all-to-all-done.1 = bf16[8,128,256]{1,2,0:T(8,128)(2,1)S(1)} async-done(((bf16[8,128,256]{1,2,0:T(8,128)(2,1)}), bf16[8,128,256]{1,2,0:T(8,128)(2,1)S(1)}, u32[]{:S(2)}, u32[]{:S(2)}) %all-to-all-start.1) | async-done | bytes 524320 | tf_op jit(solution)/shard_map/all_to_all | solution.py:145
  (68 shorter events, 11.0 us)
Async XLA Ops:
  0.6 1.9 %copy-start = (bf16[128,16]{0,1:T(8,128)(2,1)S(1)}, bf16[128,16]{0,1:T(8,128)(2,1)}, u32[]{:S(2)}) copy-start(bf16[128,16]{0,1:T(8,128)(2,1)} %param.12) | copy-start | bytes 12292
  0.6 1.4 %copy-start.4 = (bf16[128,2048]{1,0:T(8,128)(2,1)S(1)}, bf16[128,2048]{1,0:T(8,128)(2,1)}, u32[]{:S(2)}) copy-start(bf16[128,2048]{1,0:T(8,128)(2,1)} %param.10) | copy-start | bytes 1572868
  0.7 1.4 %copy-start.5 = (bf16[128,2048]{1,0:T(8,128)(2,1)S(1)}, bf16[128,2048]{1,0:T(8,128)(2,1)}, u32[]{:S(2)}) copy-start(bf16[128,2048]{1,0:T(8,128)(2,1)} %param.11) | copy-start | bytes 1572868
  4.2 33.4 %all-to-all-start = ((bf16[128,8,514]{0,2,1:T(8,128)(2,1)}), bf16[128,8,514]{0,2,1:T(8,128)(2,1)S(1)}, u32[]{:S(2)}, u32[]{:S(2)}) async-start(bf16[128,8,514]{0,2,1:T(8,128)(2,1)} %pad_maximum_fusion.4), calls=%async_computation | async-start | bytes 2129920 | tf_op jit(solution)/shard_map/all_to_all | solution.py:121
  38.1 1.0 copy-start.3
  44.1 3.2 %copy-start.1 = (bf16[8,1,128,2,128]{2,4,1,0,3:T(8,128)(2,1)S(1)}, bf16[8,1,128,2,128]{2,4,1,0,3:T(8,128)(2,1)}, u32[]{:S(2)}) copy-start(bf16[8,1,128,2,128]{2,4,1,0,3:T(8,128)(2,1)} %get-tuple-element.270) | copy-start | bytes 1572868 | tf_op jit(solution)/shard_map/while
  44.1 3.2 %copy-start.2 = (bf16[8,1,128,2,128]{2,4,1,0,3:T(8,128)(2,1)S(1)}, bf16[8,1,128,2,128]{2,4,1,0,3:T(8,128)(2,1)}, u32[]{:S(2)}) copy-start(bf16[8,1,128,2,128]{2,4,1,0,3:T(8,128)(2,1)} %get-tuple-element.271) | copy-start | bytes 1572868 | tf_op jit(solution)/shard_map/while
  44.2 3.1 %copy-start.6 = (bf16[8,128,2,128]{3,1,0,2:T(8,128)(2,1)S(1)}, bf16[8,128,2,128]{3,1,0,2:T(8,128)(2,1)}, u32[]{:S(2)}) copy-start(bf16[8,128,2,128]{3,1,0,2:T(8,128)(2,1)} %get-tuple-element.326) | copy-start | bytes 1572868 | tf_op jit(solution)/shard_map/while
  57.4 3.5 %copy-start.1 = (bf16[8,1,128,2,128]{2,4,1,0,3:T(8,128)(2,1)S(1)}, bf16[8,1,128,2,128]{2,4,1,0,3:T(8,128)(2,1)}, u32[]{:S(2)}) copy-start(bf16[8,1,128,2,128]{2,4,1,0,3:T(8,128)(2,1)} %get-tuple-element.270) | copy-start | bytes 1572868 | tf_op jit(solution)/shard_map/while
  57.4 3.5 %copy-start.2 = (bf16[8,1,128,2,128]{2,4,1,0,3:T(8,128)(2,1)S(1)}, bf16[8,1,128,2,128]{2,4,1,0,3:T(8,128)(2,1)}, u32[]{:S(2)}) copy-start(bf16[8,1,128,2,128]{2,4,1,0,3:T(8,128)(2,1)} %get-tuple-element.271) | copy-start | bytes 1572868 | tf_op jit(solution)/shard_map/while
  57.4 3.5 %copy-start.6 = (bf16[8,128,2,128]{3,1,0,2:T(8,128)(2,1)S(1)}, bf16[8,128,2,128]{3,1,0,2:T(8,128)(2,1)}, u32[]{:S(2)}) copy-start(bf16[8,128,2,128]{3,1,0,2:T(8,128)(2,1)} %get-tuple-element.326) | copy-start | bytes 1572868 | tf_op jit(solution)/shard_map/while
  70.0 10.1 %all-to-all-start.2 = ((f32[8,128,2]{1,2,0:T(2,128)}), f32[8,128,2]{1,2,0:T(2,128)S(1)}, u32[]{:S(2)}, u32[]{:S(2)}) async-start(f32[8,128,2]{1,2,0:T(2,128)} %multiply_bitcast_fusion), calls=%async_computation.2 | async-start | bytes 16384 | tf_op jit(solution)/shard_map/all_to_all | solution.py:147
  80.1 16.9 %all-to-all-start.1 = ((bf16[8,128,256]{1,2,0:T(8,128)(2,1)}), bf16[8,128,256]{1,2,0:T(8,128)(2,1)S(1)}, u32[]{:S(2)}, u32[]{:S(2)}) async-start(bf16[8,128,256]{1,2,0:T(8,128)(2,1)} %copy_bitcast_fusion.3), calls=%async_computation.1 | async-start | bytes 1048576 | tf_op jit(solution)/shard_map/all_to_all | solution.py:145
where the time goes:
time: 99.2 us; the launch traced here: 98.7 us
  waiting for transfers between devices  43.2 us (44%)
  local copies, waits for them, and re-layouts  25.7 us (26%)
  starting transfers between devices  14.4 us (15%)
  matrix products  8.83 us (9%)
  other arithmetic  5.49 us (6%)
    all_to_all x1, waiting for transfers between devices, per_device(): lax.all_to_all(packed, 'seq', split_axis=1, concat_axis=0, tiled=True)  25.4 us
    all_to_all x1, waiting for transfers between devices, per_device(): lax.all_to_all(local_grad, 'seq', split_axis=0, concat_axis=1, tiled=True)  13.4 us
    all_to_all x1, starting transfers between devices, per_device(): lax.all_to_all(packed, 'seq', split_axis=1, concat_axis=0, tiled=True)  7.28 us
    dot_general x2, matrix products, advance(): jnp.einsum('kfts,iktfg->isfg', toeplitz, stacked, preferred_element_type=...  6.6 us
    reshape x2, local copies, waits for them, and re-layouts, diagonal_sums(): trimmed.reshape(products.shape[0], products.shape[1], block_rows, 2 * blo...  5.62 us
    unnamed x17, local copies, waits for them, and re-layouts  5.54 us
    all_to_all x1, waiting for transfers between devices, per_device(): lax.all_to_all(stretch_term.reshape(seq_count, block_rows, stretch_filter...  4.37 us
    all_to_all x1, starting transfers between devices, per_device(): lax.all_to_all(stretch_term.reshape(seq_count, block_rows, stretch_filter...  3.59 us
  transfers between devices with their start and end apart: 3, of which 3 were waited for; matrix products, arithmetic and copies ran while one was open for 3% of the time, Pallas kernels for 0%

commit v1 on v0

--- a/solution.py
+++ b/solution.py
@@ -6,6 +6,29 @@
 from jax.sharding import PartitionSpec as P
 
 lag_group = 4
+
+
+def in_blocks(shard, dim, count):
+    dims = shard.shape
+    blocks = shard.reshape(*dims[:dim], count, dims[dim] // count, *dims[dim + 1 :])
+    return jnp.moveaxis(blocks, dim, 0)
+
+
+def laid_out(blocks, dim):
+    shape = list(blocks.shape[1:])
+    shape[dim] *= blocks.shape[0]
+    return jnp.moveaxis(blocks, 0, dim).reshape(shape)
+
+
+def sent_to_each(value, axis, split_dim, concat_dim):
+    peers, index = (lax.axis_size(axis), lax.axis_index(axis))
+    parts = in_blocks(value, split_dim, peers)
+    finished = [parts[index]]
+    for step in range(1, peers):
+        sent = parts[(index + step) % peers]
+        finished.append(lax.ppermute(sent, axis, [(i, (i + step) % peers) for i in range(peers)]))
+    parts = jnp.stack(finished)[(index - jnp.arange(peers)) % peers]
+    return laid_out(parts, concat_dim)
 
 
 def toeplitz_blocks(windows, block_rows):
@@ -142,7 +165,7 @@
     local_grad = (conv_grad + stretch_gain[None, :] * moved_grad.astype(jnp.float32)).astype(
         jnp.bfloat16
     )
-    input_grad = lax.all_to_all(local_grad, "seq", split_axis=0, concat_axis=1, tiled=True)
+    input_grad = sent_to_each(local_grad, "seq", 0, 1)
     stretch_term = jnp.transpose(lag_acc[:, block_rows : block_rows + length]) * taps_scale
     lag_parts = lax.all_to_all(
         stretch_term.reshape(seq_count, block_rows, stretch_filters),

time: 99.2 us -> 94.8 us (0.956)
  waiting for transfers between devices: 43.2 us -> 28.1 us
  starting transfers between devices: 14.4 us -> 24.6 us
  local copies, waits for them, and re-layouts: 25.7 us -> 27 us
    all_to_all x1 -> x0, waiting for transfers between devices: 13.4 us -> none  [per_device(): lax.all_to_all(local_grad, 'seq', split_axis=0, concat_axis=1, tiled=True)]
    ppermute x0 -> x7, starting transfers between devices: none -> 12.7 us  [sent_to_each(): lax.ppermute(sent, axis, [(i, (i + step) % peers) for i in range(peers)])]
    all_to_all x1, waiting for transfers between devices: 4.37 us -> 0.01 us  [per_device(): lax.all_to_all(stretch_term.reshape(seq_count, block_rows, stretch_filter...]
    all_to_all x1 -> x0, starting transfers between devices: 3.49 us -> none  [per_device(): lax.all_to_all(local_grad, 'seq', split_axis=0, concat_axis=1, tiled=True)]
    ppermute x0 -> x7, waiting for transfers between devices: none -> 2.75 us  [sent_to_each(): lax.ppermute(sent, axis, [(i, (i + step) % peers) for i in range(peers)])]
    all_to_all x1 -> x0, other arithmetic: 2.14 us -> none  [per_device(): lax.all_to_all(local_grad, 'seq', split_axis=0, concat_axis=1, tiled=True)]
    convert_element_type x0 -> x1, other arithmetic: none -> 1.32 us  [per_device(): (conv_grad + stretch_gain[None, :] * moved_grad.astype(jnp.float32)).asty...]
    unnamed x17 -> x23, local copies, waits for them, and re-layouts: 5.54 us -> 5.6 us
  transfers between devices with their start and end apart: 3 -> 9, of which waited for: 3 -> 4; matrix products, arithmetic and copies ran while one was open for 3% -> 1% of each run, Pallas kernels for 0% -> 0%
where the time goes in v1:
time: 94.8 us; the launch traced here: 94.3 us
  waiting for transfers between devices  28.1 us (30%)
  local copies, waits for them, and re-layouts  27 us (28%)
  starting transfers between devices  24.6 us (26%)
  matrix products  8.8 us (9%)
  other arithmetic  4.7 us (5%)
    all_to_all x1, waiting for transfers between devices, per_device(): lax.all_to_all(packed, 'seq', split_axis=1, concat_axis=0, tiled=True)  25.3 us
    ppermute x7, starting transfers between devices, sent_to_each(): lax.ppermute(sent, axis, [(i, (i + step) % peers) for i in range(peers)])  12.7 us
    all_to_all x1, starting transfers between devices, per_device(): lax.all_to_all(packed, 'seq', split_axis=1, concat_axis=0, tiled=True)  7.28 us
    dot_general x2, matrix products, advance(): jnp.einsum('kfts,iktfg->isfg', toeplitz, stacked, preferred_element_type=...  6.56 us
    reshape x2, local copies, waits for them, and re-layouts, diagonal_sums(): trimmed.reshape(products.shape[0], products.shape[1], block_rows, 2 * blo...  5.62 us
    unnamed x23, local copies, waits for them, and re-layouts  5.6 us
    all_to_all x1, starting transfers between devices, per_device(): lax.all_to_all(stretch_term.reshape(seq_count, block_rows, stretch_filter...  4.58 us
    reshape x2, local copies, waits for them, and re-layouts, toeplitz_blocks(): trimmed.reshape(windows.shape[0], windows.shape[1], block_rows, 2 * block...  3.14 us
  transfers between devices with their start and end apart: 9, of which 4 were waited for; matrix products, arithmetic and copies ran while one was open for 1% of the time, Pallas kernels for 0%

profile of v1, /device:TPU:0, one launch (start us, length us, event | category | flops | bytes accessed | tf_op | source)
XLA Modules:
  0.0 94.3 jit_solution(16122392944701335439)
XLA Ops:
  0.7 1.4 %copy.44 = bf16[128,2048]{0,1:T(8,128)(2,1)S(1)} copy(bf16[128,2048]{1,0:T(8,128)(2,1)} %param.9) | data formatting | bytes 1048576 | tf_op args[0]
  4.2 7.3 %all-to-all-start = ((bf16[128,8,514]{0,2,1:T(8,128)(2,1)}), bf16[128,8,514]{0,2,1:T(8,128)(2,1)S(1)}, u32[]{:S(2)}, u32[]{:S(2)}) async-start(bf16[128,8,514]{0,2,1:T(8,128)(2,1)} %pad_maximum_fusion.4), calls=%async_computation | async-start | bytes 2129920 | tf_op jit(solution)/shard_map/all_to_all | solution.py:144
  12.2 25.3 %all-to-all-done = bf16[128,8,514]{0,2,1:T(8,128)(2,1)S(1)} async-done(((bf16[128,8,514]{0,2,1:T(8,128)(2,1)}), bf16[128,8,514]{0,2,1:T(8,128)(2,1)S(1)}, u32[]{:S(2)}, u32[]{:S(2)}) %all-to-all-start) | async-done | bytes 1052704 | tf_op jit(solution)/shard_map/all_to_all | solution.py:144
  39.5 1.1 %copy.47 = bf16[8,128,2,128]{3,1,0,2:T(8,128)(2,1)} copy(bf16[8,128,2,128]{1,0,3,2:T(8,128)(2,1)S(1)} %bitcast.158) | data formatting | bytes 1048576
  40.7 26.9 %while.18 = (s32[]{:T(128)}, f32[8,128,2,128]{1,3,0,2:T(8,128)}, f32[2,1664]{1,0:T(2,128)S(1)}, bf16[19,128,2,128]{1,3,0,2:T(8,128)(2,1)S(1)}, bf16[2,1664]{1,0:...) while((s32[]{:T(128)}, f32[8,128,2,128]{1,3,0,2:T(8,128)}, ...), condition=%wide.region_2.3_spmd.clone, body=%wide.region_0.2_spmd.clone.sunk | while | flops 543954432 | bytes 31783416 | solution.py:109
  40.7 1.2 %dynamic-slice_bitcast_fusion.12 = (bf16[8,1,128,2,128]{2,4,1,0,3:T(8,128)(2,1)S(1)}, bf16[8,1,128,2,128]{2,4,1,0,3:T(8,128)(2,1)S(1)}, bf16[8,1,128,2,128]{2,4,1,0,3:T(8,128)(2,1)}, bf16[8,1,128,2,128]{2,4,1,0,3:T(8,128)(2,1)}) fusion(bf16[19,128,2,128]{1,3,0,2:T(8,128)(2,1)S(1)} %get-tuple-element.340, s32[]{:T(128)S(6)} %select_n.173, ...), kind=kLoop, calls=%fused_computation.10.clone.1 | loop fusion | bytes 4194320 | tf_op jit(solution)/shard_map/while/body/eval_jaxpr/stack | solution.py:72
  42.6 1.6 %reshape.169 = bf16[4,2,128,255]{3,2,1,0:T(8,128)(2,1)S(1)} reshape(bf16[4,2,32640]{2,1,0:T(2,128)(2,1)S(1)} %slice.145) | data formatting | bytes 1044480 | tf_op jit(solution)/shard_map/while/body/eval_jaxpr/reshape | solution.py:38
  44.2 3.1 %fusion.21 = f32[8,128,2,128]{1,3,0,2:T(8,128)} fusion(f32[8,128,2,128]{1,3,0,2:T(8,128)} %get-tuple-element.317, pred[]{:T(512)S(6)} %compare.23, bf16[8,1,128,2,128]{2,4,1,0,3:T(8,128)(2,1)S(1)} %get-tuple-element.285, bf16[8,1,128,2,128]{2,4,1,0,3:T(8,128)(2,1)} %get-tuple-element.286, bf16[8,1,128,2,128]{2,4,1,0,3:T(8,128)(2,1)} %get-tuple-element.287, ...), kind=kOutput, calls=%fused_computation.4.clone.1 | convolution fusion | flops 272105472 | bytes 4456449 | tf_op jit(solution)/shard_map/while/body/eval_jaxpr/kfts,iktfg->isfg/dot_general | solution.py:90
  47.4 1.1 %convolution_bitcast_fusion.3 = f32[4,2,128,128]{3,2,0,1:T(8,128)S(1)} fusion(bf16[8,128,2,128]{3,1,0,2:T(8,128)(2,1)S(1)} %copy-done.6, bf16[8,1,128,2,128]{2,4,1,0,3:T(8,128)(2,1)S(1)} %get-tuple-element.285, bf16[8,1,128,2,128]{2,4,1,0,3:T(8,128)(2,1)S(1)} %copy-done.1, bf16[8,1,128,2,128]{2,4,1,0,3:T(8,128)(2,1)S(1)} %copy-done.2, ...), kind=kOutput, calls=%fused_computation.5.clone.1 | convolution fusion | flops 271581184 | bytes 3145728 | tf_op jit(solution)/shard_map/while/body/eval_jaxpr/iktfg,isfg->kfts/dot_general | solution.py:93
  50.9 2.8 %reshape.171 = f32[4,2,128,255]{3,2,0,1:T(8,128)S(1)} reshape(f32[4,2,32640]{2,0,1:T(4,128)} %slice.146) | data formatting | bytes 2088960 | tf_op jit(solution)/shard_map/while/body/eval_jaxpr/reshape | solution.py:47
  53.9 1.2 %dynamic-slice_bitcast_fusion.12 = (bf16[8,1,128,2,128]{2,4,1,0,3:T(8,128)(2,1)S(1)}, bf16[8,1,128,2,128]{2,4,1,0,3:T(8,128)(2,1)S(1)}, bf16[8,1,128,2,128]{2,4,1,0,3:T(8,128)(2,1)}, bf16[8,1,128,2,128]{2,4,1,0,3:T(8,128)(2,1)}) fusion(bf16[19,128,2,128]{1,3,0,2:T(8,128)(2,1)S(1)} %get-tuple-element.340, s32[]{:T(128)S(6)} %select_n.173, ...), kind=kLoop, calls=%fused_computation.10.clone.1 | loop fusion | bytes 4194320 | tf_op jit(solution)/shard_map/while/body/eval_jaxpr/stack | solution.py:72
  55.9 1.6 %reshape.169 = bf16[4,2,128,255]{3,2,1,0:T(8,128)(2,1)S(1)} reshape(bf16[4,2,32640]{2,1,0:T(2,128)(2,1)S(1)} %slice.145) | data formatting | bytes 1044480 | tf_op jit(solution)/shard_map/while/body/eval_jaxpr/reshape | solution.py:38
  57.5 3.5 %fusion.21 = f32[8,128,2,128]{1,3,0,2:T(8,128)} fusion(f32[8,128,2,128]{1,3,0,2:T(8,128)} %get-tuple-element.317, pred[]{:T(512)S(6)} %compare.23, bf16[8,1,128,2,128]{2,4,1,0,3:T(8,128)(2,1)S(1)} %get-tuple-element.285, bf16[8,1,128,2,128]{2,4,1,0,3:T(8,128)(2,1)} %get-tuple-element.286, bf16[8,1,128,2,128]{2,4,1,0,3:T(8,128)(2,1)} %get-tuple-element.287, ...), kind=kOutput, calls=%fused_computation.4.clone.1 | convolution fusion | flops 272105472 | bytes 4456449 | tf_op jit(solution)/shard_map/while/body/eval_jaxpr/kfts,iktfg->isfg/dot_general | solution.py:90
  64.5 2.8 %reshape.171 = f32[4,2,128,255]{3,2,0,1:T(8,128)S(1)} reshape(f32[4,2,32640]{2,0,1:T(4,128)} %slice.146) | data formatting | bytes 2088960 | tf_op jit(solution)/shard_map/while/body/eval_jaxpr/reshape | solution.py:47
  67.5 1.3 %broadcast_multiply_fusion = f32[8,128,2,128]{1,3,0,2:T(8,128)S(1)} fusion(f32[8,128,2,128]{1,3,0,2:T(8,128)} %get-tuple-element.161), kind=kLoop, calls=%fused_computation.32 | loop fusion | flops 262144 | bytes 2097152 | tf_op jit(solution)/shard_map/mul | solution.py:164
  69.5 1.3 %fusion.9 = bf16[1024,256]{0,1:T(8,128)(2,1)S(1)} fusion(f32[32,8,8,128]{3,2,1,0:T(8,128)S(1)} %bitcast.154, f32[256]{0:T(256)S(1)} %dynamic_slice.87, bf16[1024,514]{0,1:T(8,128)(2,1)} %bitcast.150), kind=kLoop, calls=%fused_computation.29 | loop fusion | flops 1048576 | bytes 2098176 | tf_op jit(solution)/shard_map/convert_element_type | solution.py:165
  71.1 1.5 %collective-permute-start = (bf16[128,256]{1,0:T(8,128)(2,1)S(1)}, bf16[128,256]{1,0:T(8,128)(2,1)S(1)}, u32[]{:S(2)}, u32[]{:S(2)}) collective-permute-start(bf16[128,256]{1,0:T(8,128)(2,1)S(1)} %get-tuple-element.236), channel_id=1, source_target_pairs={{0,2},{2,4},{4,6},{6,8},{8,10},{10,12},{12,14},{14,0},{1,3},{3,5},... | collective-permute-start | bytes 196616 | tf_op jit(solution)/shard_map/ppermute | solution.py:29
  73.2 4.6 %all-to-all-start.1 = ((f32[8,128,2]{1,2,0:T(2,128)}), f32[8,128,2]{1,2,0:T(2,128)S(1)}, u32[]{:S(2)}, u32[]{:S(2)}) async-start(f32[8,128,2]{1,2,0:T(2,128)} %multiply_bitcast_fusion), calls=%async_computation.1 | async-start | bytes 16384 | tf_op jit(solution)/shard_map/all_to_all | solution.py:170
  77.7 2.1 %collective-permute-start.1 = (bf16[128,256]{1,0:T(8,128)(2,1)S(1)}, bf16[128,256]{1,0:T(8,128)(2,1)S(1)}, u32[]{:S(2)}, u32[]{:S(2)}) collective-permute-start(bf16[128,256]{1,0:T(8,128)(2,1)S(1)} %get-tuple-element.235), channel_id=1, source_target_pairs={{0,4},{2,6},{4,8},{6,10},{8,12},{10,14},{12,0},{14,2},{1,5},{3,7},... | collective-permute-start | bytes 196616 | tf_op jit(solution)/shard_map/ppermute | solution.py:29
  79.8 2.4 %collective-permute-start.2 = (bf16[128,256]{1,0:T(8,128)(2,1)S(1)}, bf16[128,256]{1,0:T(8,128)(2,1)S(1)}, u32[]{:S(2)}, u32[]{:S(2)}) collective-permute-start(bf16[128,256]{1,0:T(8,128)(2,1)S(1)} %get-tuple-element.234), channel_id=1, source_target_pairs={{0,6},{2,8},{4,10},{6,12},{8,14},{10,0},{12,2},{14,4},{1,7},{3,9},... | collective-permute-start | bytes 196616 | tf_op jit(solution)/shard_map/ppermute | solution.py:29
  82.2 1.5 %collective-permute-start.3 = (bf16[128,256]{1,0:T(8,128)(2,1)S(1)}, bf16[128,256]{1,0:T(8,128)(2,1)S(1)}, u32[]{:S(2)}, u32[]{:S(2)}) collective-permute-start(bf16[128,256]{1,0:T(8,128)(2,1)S(1)} %get-tuple-element.233), channel_id=1, source_target_pairs={{0,8},{2,10},{4,12},{6,14},{8,0},{10,2},{12,4},{14,6},{1,9},{3,11}... | collective-permute-start | bytes 196616 | tf_op jit(solution)/shard_map/ppermute | solution.py:29
  83.6 2.4 %collective-permute-start.4 = (bf16[128,256]{1,0:T(8,128)(2,1)S(1)}, bf16[128,256]{1,0:T(8,128)(2,1)S(1)}, u32[]{:S(2)}, u32[]{:S(2)}) collective-permute-start(bf16[128,256]{1,0:T(8,128)(2,1)S(1)} %get-tuple-element.232), channel_id=1, source_target_pairs={{0,10},{2,12},{4,14},{6,0},{8,2},{10,4},{12,6},{14,8},{1,11},{3,13... | collective-permute-start | bytes 196616 | tf_op jit(solution)/shard_map/ppermute | solution.py:29
  86.0 1.5 %collective-permute-start.5 = (bf16[128,256]{1,0:T(8,128)(2,1)S(1)}, bf16[128,256]{1,0:T(8,128)(2,1)S(1)}, u32[]{:S(2)}, u32[]{:S(2)}) collective-permute-start(bf16[128,256]{1,0:T(8,128)(2,1)S(1)} %get-tuple-element.231), channel_id=1, source_target_pairs={{0,12},{2,14},{4,0},{6,2},{8,4},{10,6},{12,8},{14,10},{1,13},{3,15... | collective-permute-start | bytes 196616 | tf_op jit(solution)/shard_map/ppermute | solution.py:29
  87.5 1.5 %collective-permute-start.6 = (bf16[128,256]{1,0:T(8,128)(2,1)S(1)}, bf16[128,256]{1,0:T(8,128)(2,1)S(1)}, u32[]{:S(2)}, u32[]{:S(2)}) collective-permute-start(bf16[128,256]{1,0:T(8,128)(2,1)S(1)} %get-tuple-element.230), channel_id=1, source_target_pairs={{0,14},{2,0},{4,2},{6,4},{8,6},{10,8},{12,10},{14,12},{1,15},{3,1}... | collective-permute-start | bytes 196616 | tf_op jit(solution)/shard_map/ppermute | solution.py:29
  (93 shorter events, 19.3 us)
Async XLA Ops:
  0.6 1.9 %copy-start = (bf16[128,16]{0,1:T(8,128)(2,1)S(1)}, bf16[128,16]{0,1:T(8,128)(2,1)}, u32[]{:S(2)}) copy-start(bf16[128,16]{0,1:T(8,128)(2,1)} %param.12) | copy-start | bytes 12292
  0.6 1.4 %copy-start.4 = (bf16[128,2048]{1,0:T(8,128)(2,1)S(1)}, bf16[128,2048]{1,0:T(8,128)(2,1)}, u32[]{:S(2)}) copy-start(bf16[128,2048]{1,0:T(8,128)(2,1)} %param.10) | copy-start | bytes 1572868
  0.7 1.4 %copy-start.5 = (bf16[128,2048]{1,0:T(8,128)(2,1)S(1)}, bf16[128,2048]{1,0:T(8,128)(2,1)}, u32[]{:S(2)}) copy-start(bf16[128,2048]{1,0:T(8,128)(2,1)} %param.11) | copy-start | bytes 1572868
  4.2 33.4 %all-to-all-start = ((bf16[128,8,514]{0,2,1:T(8,128)(2,1)}), bf16[128,8,514]{0,2,1:T(8,128)(2,1)S(1)}, u32[]{:S(2)}, u32[]{:S(2)}) async-start(bf16[128,8,514]{0,2,1:T(8,128)(2,1)} %pad_maximum_fusion.4), calls=%async_computation | async-start | bytes 2129920 | tf_op jit(solution)/shard_map/all_to_all | solution.py:144
  38.1 1.0 %copy-start.3 = (bf16[65,8,8,128]{3,1,2,0:T(8,128)(2,1)}, bf16[65,8,8,128]{3,1,2,0:T(8,128)(2,1)S(1)}, u32[]{:S(2)}) copy-start(bf16[65,8,8,128]{3,1,2,0:T(8,128)(2,1)S(1)} %copy.63) | copy-start | bytes 3194884
  44.2 3.1 %copy-start.1 = (bf16[8,1,128,2,128]{2,4,1,0,3:T(8,128)(2,1)S(1)}, bf16[8,1,128,2,128]{2,4,1,0,3:T(8,128)(2,1)}, u32[]{:S(2)}) copy-start(bf16[8,1,128,2,128]{2,4,1,0,3:T(8,128)(2,1)} %get-tuple-element.286) | copy-start | bytes 1572868 | tf_op jit(solution)/shard_map/while
  44.2 3.1 %copy-start.2 = (bf16[8,1,128,2,128]{2,4,1,0,3:T(8,128)(2,1)S(1)}, bf16[8,1,128,2,128]{2,4,1,0,3:T(8,128)(2,1)}, u32[]{:S(2)}) copy-start(bf16[8,1,128,2,128]{2,4,1,0,3:T(8,128)(2,1)} %get-tuple-element.287) | copy-start | bytes 1572868 | tf_op jit(solution)/shard_map/while
  44.2 3.1 %copy-start.6 = (bf16[8,128,2,128]{3,1,0,2:T(8,128)(2,1)S(1)}, bf16[8,128,2,128]{3,1,0,2:T(8,128)(2,1)}, u32[]{:S(2)}) copy-start(bf16[8,128,2,128]{3,1,0,2:T(8,128)(2,1)} %get-tuple-element.342) | copy-start | bytes 1572868 | tf_op jit(solution)/shard_map/while
  57.5 3.5 %copy-start.1 = (bf16[8,1,128,2,128]{2,4,1,0,3:T(8,128)(2,1)S(1)}, bf16[8,1,128,2,128]{2,4,1,0,3:T(8,128)(2,1)}, u32[]{:S(2)}) copy-start(bf16[8,1,128,2,128]{2,4,1,0,3:T(8,128)(2,1)} %get-tuple-element.286) | copy-start | bytes 1572868 | tf_op jit(solution)/shard_map/while
  57.5 3.5 %copy-start.2 = (bf16[8,1,128,2,128]{2,4,1,0,3:T(8,128)(2,1)S(1)}, bf16[8,1,128,2,128]{2,4,1,0,3:T(8,128)(2,1)}, u32[]{:S(2)}) copy-start(bf16[8,1,128,2,128]{2,4,1,0,3:T(8,128)(2,1)} %get-tuple-element.287) | copy-start | bytes 1572868 | tf_op jit(solution)/shard_map/while
  57.5 3.5 %copy-start.6 = (bf16[8,128,2,128]{3,1,0,2:T(8,128)(2,1)S(1)}, bf16[8,128,2,128]{3,1,0,2:T(8,128)(2,1)}, u32[]{:S(2)}) copy-start(bf16[8,128,2,128]{3,1,0,2:T(8,128)(2,1)} %get-tuple-element.342) | copy-start | bytes 1572868 | tf_op jit(solution)/shard_map/while
  71.1 14.9 %collective-permute-start = (bf16[128,256]{1,0:T(8,128)(2,1)S(1)}, bf16[128,256]{1,0:T(8,128)(2,1)S(1)}, u32[]{:S(2)}, u32[]{:S(2)}) collective-permute-start(bf16[128,256]{1,0:T(8,128)(2,1)S(1)} %get-tuple-element.236), channel_id=1, source_target_pairs={{0,2},{2,4},{4,6},{6,8},{8,10},{10,12},{12,14},{14,0},{1,3},{3,5},... | collective-permute-start | bytes 196616 | tf_op jit(solution)/shard_map/ppermute | solution.py:29
  73.2 12.9 %all-to-all-start.1 = ((f32[8,128,2]{1,2,0:T(2,128)}), f32[8,128,2]{1,2,0:T(2,128)S(1)}, u32[]{:S(2)}, u32[]{:S(2)}) async-start(f32[8,128,2]{1,2,0:T(2,128)} %multiply_bitcast_fusion), calls=%async_computation.1 | async-start | bytes 16384 | tf_op jit(solution)/shard_map/all_to_all | solution.py:170
  77.7 9.7 %collective-permute-start.1 = (bf16[128,256]{1,0:T(8,128)(2,1)S(1)}, bf16[128,256]{1,0:T(8,128)(2,1)S(1)}, u32[]{:S(2)}, u32[]{:S(2)}) collective-permute-start(bf16[128,256]{1,0:T(8,128)(2,1)S(1)} %get-tuple-element.235), channel_id=1, source_target_pairs={{0,4},{2,6},{4,8},{6,10},{8,12},{10,14},{12,0},{14,2},{1,5},{3,7},... | collective-permute-start | bytes 196616 | tf_op jit(solution)/shard_map/ppermute | solution.py:29
  79.8 9.2 %collective-permute-start.2 = (bf16[128,256]{1,0:T(8,128)(2,1)S(1)}, bf16[128,256]{1,0:T(8,128)(2,1)S(1)}, u32[]{:S(2)}, u32[]{:S(2)}) collective-permute-start(bf16[128,256]{1,0:T(8,128)(2,1)S(1)} %get-tuple-element.234), channel_id=1, source_target_pairs={{0,6},{2,8},{4,10},{6,12},{8,14},{10,0},{12,2},{14,4},{1,7},{3,9},... | collective-permute-start | bytes 196616 | tf_op jit(solution)/shard_map/ppermute | solution.py:29
  82.2 7.8 %collective-permute-start.3 = (bf16[128,256]{1,0:T(8,128)(2,1)S(1)}, bf16[128,256]{1,0:T(8,128)(2,1)S(1)}, u32[]{:S(2)}, u32[]{:S(2)}) collective-permute-start(bf16[128,256]{1,0:T(8,128)(2,1)S(1)} %get-tuple-element.233), channel_id=1, source_target_pairs={{0,8},{2,10},{4,12},{6,14},{8,0},{10,2},{12,4},{14,6},{1,9},{3,11}... | collective-permute-start | bytes 196616 | tf_op jit(solution)/shard_map/ppermute | solution.py:29
  83.6 6.3 %collective-permute-start.4 = (bf16[128,256]{1,0:T(8,128)(2,1)S(1)}, bf16[128,256]{1,0:T(8,128)(2,1)S(1)}, u32[]{:S(2)}, u32[]{:S(2)}) collective-permute-start(bf16[128,256]{1,0:T(8,128)(2,1)S(1)} %get-tuple-element.232), channel_id=1, source_target_pairs={{0,10},{2,12},{4,14},{6,0},{8,2},{10,4},{12,6},{14,8},{1,11},{3,13... | collective-permute-start | bytes 196616 | tf_op jit(solution)/shard_map/ppermute | solution.py:29
  86.0 4.7 %collective-permute-start.5 = (bf16[128,256]{1,0:T(8,128)(2,1)S(1)}, bf16[128,256]{1,0:T(8,128)(2,1)S(1)}, u32[]{:S(2)}, u32[]{:S(2)}) collective-permute-start(bf16[128,256]{1,0:T(8,128)(2,1)S(1)} %get-tuple-element.231), channel_id=1, source_target_pairs={{0,12},{2,14},{4,0},{6,2},{8,4},{10,6},{12,8},{14,10},{1,13},{3,15... | collective-permute-start | bytes 196616 | tf_op jit(solution)/shard_map/ppermute | solution.py:29
  87.5 4.3 %collective-permute-start.6 = (bf16[128,256]{1,0:T(8,128)(2,1)S(1)}, bf16[128,256]{1,0:T(8,128)(2,1)S(1)}, u32[]{:S(2)}, u32[]{:S(2)}) collective-permute-start(bf16[128,256]{1,0:T(8,128)(2,1)S(1)} %get-tuple-element.230), channel_id=1, source_target_pairs={{0,14},{2,0},{4,2},{6,4},{8,6},{10,8},{12,10},{14,12},{1,15},{3,1}... | collective-permute-start | bytes 196616 | tf_op jit(solution)/shard_map/ppermute | solution.py:29
